TPU v7x, 256 devices: a whole 4x4x8 slice. The times are simulated.
256 devices in a mesh: row: 4 (over y), col: 4 (over x), dp: 16 (over z, core).
Axes of the slice: x: 4, y: 4, z: 8, core: 2. Of those that a mesh axis runs over, the one named last changes fastest.
Arguments:
- hidden_states: bfloat16 [16384, 1536], P(('dp', 'row'), 'col'), may hold values from -18 to 18
- w_query: bfloat16 [1536, 1536], P('col', 'row'), may hold values from -0.102062073 to 0.102062073
- w_key_value: bfloat16 [1536, 512], P('col'), may hold values from -0.102062073 to 0.102062073
- adapter_down: bfloat16 [1024, 1536, 16], P('dp', 'col'), may hold values from -0.15625 to 0.15625
- adapter_up: bfloat16 [1024, 16, 1536], P('dp', None, 'row'), may hold values from -1.5 to 1.5
- req_lengths: int32 [16, 8], replicated, may hold values from 1 to 160, 960 in all within a row
- req_adapter: int32 [16, 8], replicated, may hold values from 0 to 1023, as said below
Outputs:
- attention: bfloat16 [16384, 1536], P(('dp', 'col'), 'row')
- kv_cache: bfloat16 [16384, 512], P(('dp', 'col'))
Inputs may be any that keep to these rules, and one draw needn't show every extreme that they name: `req_lengths`: the lengths of one block sum to 960, and each block has a request of exactly 160 tokens. `req_adapter`: adapters k * 64 to (k + 1) * 64 - 1 are those of index k of dp; the requests of one block use adapters of one index of dp at most 1 times, and some index of dp is used exactly that often by every block.
All inputs are finite; a program needn't handle non-finite values.
Results may differ from a plain program's by a relative error of at most 0.0072.
Values may be sent and summed in bfloat16 or wider, within the bound.
No kernel may reach another device: no remote copies, remote signals or barrier semaphores. Data moves between devices by JAX's collectives and lax.ppermute only.
A program may use at most 128 MiB of HBM per device.

v0:
```python
import math
import jax
import jax.numpy as jnp
from jax import lax
from jax.sharding import PartitionSpec as P

HEAD_DIM = 128
MOST_LEN = 160
masked_score = -1e30


def block_layout(lengths_row, block_len):
    prefix_len = block_len - jnp.sum(lengths_row)
    ends_at = jnp.cumsum(lengths_row) + prefix_len
    starts = ends_at - lengths_row
    positions = jnp.arange(block_len, dtype=jnp.int32)
    segment = jnp.sum((positions[:, None] >= starts[None, :]).astype(jnp.int32), axis=1)
    return (starts, segment, positions)


def slot_numbers(holders):
    request_total = holders.shape[0]
    ordering = jnp.arange(request_total, dtype=jnp.int32)
    earlier = ordering[None, :] < ordering[:, None]
    same_holder = holders[:, None] == holders[None, :]
    return jnp.sum((earlier & same_holder).astype(jnp.int32), axis=1)


def make_attend(query_rows, segment, first_row, kv_group, head_size, kv_half):
    own_rows = query_rows.shape[0]
    heads_here = query_rows.shape[1] // head_size
    query_heads = query_rows.reshape(own_rows, heads_here, head_size)
    query_pos = first_row + jnp.arange(own_rows, dtype=jnp.int32)
    query_seg = lax.dynamic_slice_in_dim(segment, first_row, own_rows, 0)
    score_scale = 1.0 / math.sqrt(head_size)

    def attend(state_in, key_block, key_start):
        running_max, running_sum, running_out = state_in
        block_size = key_block.shape[0]
        key_rows = lax.dynamic_slice_in_dim(key_block, kv_group * head_size, head_size, 1)
        values = lax.dynamic_slice_in_dim(key_block, kv_half + kv_group * head_size, head_size, 1)
        key_pos = jnp.arange(block_size, dtype=jnp.int32)
        allowed = (key_pos[None, :] <= query_pos[:, None]) & (
            (segment[None, :] == query_seg[:, None]) | (segment[None, :] == 0)
        )
        scores = (
            jnp.einsum("qhd,kd->hqk", query_heads, key_rows, preferred_element_type=jnp.float32)
            * score_scale
        )
        scores = jnp.where(allowed[None], scores, masked_score)
        new_max = jnp.maximum(running_max, jnp.max(scores, axis=2))
        weights = jnp.where(allowed[None], jnp.exp(scores - new_max[:, :, None]), 0.0)
        running_sum = jnp.sum(weights, axis=2)
        running_out = jnp.einsum(
            "hqk,kd->hqd", weights.astype(jnp.bfloat16), values, preferred_element_type=jnp.float32
        )
        return (new_max, running_sum, running_out)

    initial = (
        jnp.full((heads_here, own_rows), masked_score, jnp.float32),
        jnp.zeros((heads_here, own_rows), jnp.float32),
        jnp.zeros((heads_here, own_rows, head_size), jnp.float32),
    )
    return (attend, initial)


def body(hidden_states, w_query, w_key_value, adapter_down, adapter_up, req_lengths, req_adapter):
    dp_size = lax.axis_size("dp")
    block_index = lax.axis_index("dp")
    col_index = lax.axis_index("col")
    row_index = lax.axis_index("row")
    gathered = lax.all_gather(hidden_states, "row", axis=0, tiled=True)
    block_len = gathered.shape[0]
    query_cols = w_query.shape[1]
    kv_cols = w_key_value.shape[1]
    kv_half = kv_cols // 2
    head_size = HEAD_DIM
    heads_here = query_cols // head_size
    heads_total = heads_here * lax.axis_size("row")
    kv_heads = kv_half // head_size
    kv_group = row_index * heads_here // (heads_total // kv_heads)
    own_rows = block_len // lax.axis_size("col")
    first_row = col_index * own_rows
    held_sets = adapter_down.shape[0]
    width_here = adapter_down.shape[1]
    rank_size = adapter_down.shape[2]
    lengths_row = req_lengths[block_index]
    adapters_row = req_adapter[block_index]
    requests = lengths_row.shape[0]
    starts, segment, positions = block_layout(lengths_row, block_len)
    request_of = jnp.clip(segment - 1, 0, requests - 1)
    in_request = segment > 0
    holders = adapters_row // held_sets
    wanted_from_me = req_adapter // held_sets == block_index
    local_pick = jnp.sum(jnp.where(wanted_from_me, req_adapter % held_sets, 0), axis=1)
    down_pick = jnp.transpose(jnp.take(adapter_down, local_pick, axis=0), (0, 2, 1))
    up_pick = jnp.take(adapter_up, local_pick, axis=0)
    outgoing = jnp.concatenate([down_pick, up_pick], axis=1)
    incoming = lax.all_to_all(outgoing, "dp", split_axis=0, concat_axis=0, tiled=True)
    flat_down = incoming[:, :rank_size, :].reshape(dp_size * rank_size, width_here).T
    flat_up = (
        incoming[:, rank_size:, :].reshape(dp_size * rank_size, query_cols).astype(jnp.float32)
    )
    rank_owner = jnp.arange(dp_size * rank_size, dtype=jnp.int32) // rank_size
    reduced = jnp.dot(gathered, flat_down, preferred_element_type=jnp.float32)
    request_ids = jnp.arange(requests, dtype=jnp.int32)
    token_holder = (
        jnp.sum(
            jnp.where(segment[:, None] == request_ids[None, :] + 1, holders[None, :] + 1, 0), axis=1
        )
        - 1
    )
    kept_cols = rank_owner[None, :] == token_holder[:, None]
    reduced = jnp.where(kept_cols, reduced, 0.0)
    adapter_term = jnp.dot(reduced, flat_up, precision=lax.Precision.HIGHEST)
    kv_share = kv_cols // lax.axis_size("row")
    kv_slice = lax.dynamic_slice_in_dim(w_key_value, row_index * kv_share, kv_share, 1)
    both_weights = jnp.concatenate([w_query, kv_slice], axis=1)
    partial_value = jnp.dot(gathered, both_weights, preferred_element_type=jnp.float32)
    summed = lax.psum_scatter(
        partial_value
        + jnp.concatenate(
            [adapter_term, jnp.zeros((own_rows * lax.axis_size("col"), kv_share), jnp.float32)],
            axis=1,
        ),
        "col",
        scatter_dimension=0,
        tiled=True,
    )
    query_rows = summed[:, :query_cols].astype(jnp.bfloat16)
    kv_pieces = lax.all_gather(summed[:, query_cols:].astype(jnp.bfloat16), ("row", "col"), axis=0)
    kv_pieces = kv_pieces.reshape(lax.axis_size("row"), lax.axis_size("col"), own_rows, kv_share)
    own_pieces = lax.dynamic_index_in_dim(kv_pieces, col_index, 1, keepdims=False)
    kv_cache = jnp.transpose(own_pieces, (1, 0, 2)).reshape(own_rows, kv_cols)
    parts_per_head = head_size // kv_share
    key_all = lax.dynamic_slice_in_dim(kv_pieces, kv_group * parts_per_head, parts_per_head, 0)
    value_all = lax.dynamic_slice_in_dim(
        kv_pieces, (kv_heads + kv_group) * parts_per_head, parts_per_head, 0
    )
    key_all = jnp.transpose(key_all, (1, 2, 0, 3)).reshape(block_len, head_size)
    value_all = jnp.transpose(value_all, (1, 2, 0, 3)).reshape(block_len, head_size)
    attend, initial = make_attend(query_rows, segment, first_row, 0, head_size, head_size)
    running_max, running_sum, running_out = attend(
        initial, jnp.concatenate([key_all, value_all], axis=1), jnp.int32(0)
    )
    attention = (running_out / running_sum[:, :, None]).astype(jnp.bfloat16)
    attention = jnp.transpose(attention, (1, 0, 2)).reshape(own_rows, query_cols)
    return (attention, kv_cache)


def solution(mesh):
    return jax.shard_map(
        body,
        mesh=mesh,
        in_specs=(
            P(("dp", "row"), "col"),
            P("col", "row"),
            P("col", None),
            P("dp", "col", None),
            P("dp", None, "row"),
            P(),
            P(),
        ),
        out_specs=(P(("dp", "col"), "row"), P(("dp", "col"), None)),
        check_vma=False,
    )
```

profile of v0, /device:TPU:2, one launch (start us, length us, event | category | flops | bytes accessed | tf_op | source)
XLA Modules:
  0.0 139.3 jit_solution(9572171960682573029)
XLA Ops:
  7.2 0.8 fusion.25
  8.0 0.3 copy-done
  8.3 0.6 gather_fusion.1
  8.9 1.7 %gather_fusion = bf16[16,384,16]{1,2,0:T(8,128)(2,1)S(1)} fusion(bf16[64,384,16]{1,2,0:T(8,128)(2,1)} %param.10, s32[1024]{0:T(1024)S(1)} %pad_clamp_fusion), kind=kCustom, calls=%fused_computation | custom fusion | bytes 393280 | tf_op jit(solution)/shard_map/jit(_take)/gather | solution.py:96
  10.9 0.8 pad_maximum_fusion
  11.6 8.6 %all-to-all-start = ((bf16[16,32,384]{2,1,0:T(8,128)(2,1)}), bf16[16,32,384]{2,1,0:T(8,128)(2,1)S(1)}, u32[]{:S(2)}, u32[]{:S(2)}) async-start(bf16[16,32,384]{2,1,0:T(8,128)(2,1)} %pad_maximum_fusion), calls=%async_computation | async-start | bytes 786432 | tf_op jit(solution)/shard_map/all_to_all | solution.py:99
  20.3 0.7 fusion.34
  21.9 0.9 constant_dynamic-slice_fusion.3
  22.9 14.5 %all_gather.9 = bf16[1024,384]{1,0:T(8,128)(2,1)S(1)} all-gather(bf16[256,384]{1,0:T(8,128)(2,1)S(1)} %copy-done.2), channel_id=1, replica_groups=mesh['row'=4,'col'=4,'dp'=16] {'row'}, dimensions={0}, use_global_device_ids=true | all-gather | bytes 983040 | tf_op jit(solution)/shard_map/all_gather | solution.py:72
  37.4 0.5 fusion.6
  37.9 0.9 fusion.36
  38.8 2.1 %bitcast_add_fusion = f32[1024,512]{0,1:T(8,128)} fusion(f32[1024,384]{0,1:T(8,128)S(1)} %fusion.36, bf16[1024,384]{1,0:T(8,128)(2,1)S(1)} %all_gather.9, bf16[384,128]{1,0:T(8,128)(2,1)S(1)} %constant_dynamic-slice_fusion.3, bf16[384,384]{1,0:T(8,128)(2,1)S(1)} %copy-done.1), kind=kOutput, calls=%fused_computation.7 | convolution fusion | flops 403963904 | bytes 4849664 | tf_op jit(solution)/shard_map/dot_general | solution.py:119
  41.0 32.3 %reduce-scatter.2.cloned.1.call-done = f32[256,512]{0,1:T(8,128)} async-done(((f32[1024,512]{0,1:T(8,128)}), f32[256,512]{0,1:T(8,128)}) %reduce-scatter.2.cloned.1.call-update) | async-done | bytes 524304 | tf_op jit(solution)/shard_map/reduce_scatter | solution.py:120
  73.3 1.1 convert.4
  74.4 0.6 slice.24
  75.2 0.8 fusion.10
  76.0 49.1 %all-gather.3.cloned.1.call-done = bf16[4096,128]{0,1:T(8,128)(2,1)} async-done(((bf16[256,128]{0,1:T(8,128)(2,1)}), bf16[4096,128]{0,1:T(8,128)(2,1)}) %all-gather.3.cloned.1.call-update) | async-done | bytes 1048592 | tf_op jit(solution)/shard_map/all_gather | solution.py:131
  125.1 1.8 %reshape.151 = bf16[4,4,256,128]{2,1,0,3:T(4,128)(2,1)S(1)} reshape(bf16[4096,128]{0,1:T(8,128)(2,1)} %all-gather.3.cloned.1.call-done) | data formatting | bytes 2097152 | tf_op jit(solution)/shard_map/reshape | solution.py:132
  127.0 0.5 constant_dynamic-slice_fusion.2
  127.6 0.8 copy.35
  129.1 0.7 fusion
  129.8 0.8 fusion.1
  130.6 1.0 fusion.14
  131.6 0.8 copy.34
  (36 shorter events, 1.5 us)
Async XLA Ops:
  7.2 1.2 copy-start
  7.2 13.1 %copy-start.3 = (s32[16,8]{0,1:T(8,128)S(1)}, s32[16,8]{0,1:T(8,128)}, u32[]{:S(2)}) copy-start(s32[16,8]{0,1:T(8,128)} %param.13) | copy-start | bytes 1540
  7.2 13.1 %copy-start.4 = (s32[16,8]{0,1:T(8,128)S(1)}, s32[16,8]{0,1:T(8,128)}, u32[]{:S(2)}) copy-start(s32[16,8]{0,1:T(8,128)} %param.12) | copy-start | bytes 1540
  7.2 15.7 %copy-start.2 = (bf16[256,384]{1,0:T(8,128)(2,1)S(1)}, bf16[256,384]{1,0:T(8,128)(2,1)}, u32[]{:S(2)}) copy-start(bf16[256,384]{1,0:T(8,128)(2,1)} %param.7) | copy-start | bytes 589828
  11.6 25.8 %all-to-all-start = ((bf16[16,32,384]{2,1,0:T(8,128)(2,1)}), bf16[16,32,384]{2,1,0:T(8,128)(2,1)S(1)}, u32[]{:S(2)}, u32[]{:S(2)}) async-start(bf16[16,32,384]{2,1,0:T(8,128)(2,1)} %pad_maximum_fusion), calls=%async_computation | async-start | bytes 786432 | tf_op jit(solution)/shard_map/all_to_all | solution.py:99
  20.2 53.1 %reduce-scatter.2.cloned.1.call-start = ((), (), s32[]{:S(2)}) async-start(), calls=%async_computation.2 | async-start | bytes 2621440 | tf_op jit(solution)/shard_map/reduce_scatter | solution.py:120
  22.9 15.9 %copy-start.1 = (bf16[384,384]{1,0:T(8,128)(2,1)S(1)}, bf16[384,384]{1,0:T(8,128)(2,1)}, u32[]{:S(2)}) copy-start(bf16[384,384]{1,0:T(8,128)(2,1)} %param.8) | copy-start | bytes 884740
  41.0 84.2 %all-gather.3.cloned.1.call-start = ((), (), s32[]{:S(2)}) async-start(), calls=%async_computation.3 | async-start | bytes 1114112 | tf_op jit(solution)/shard_map/all_gather | solution.py:131
Sparse Core Ops, SparseCore 0:
  41.1 32.1 reduce-scatter.1
  76.3 48.8 all-gather.2
where the time goes:
time: 140 us; the launch traced here: 139 us
  waiting for transfers between devices  81.5 us (58%)
  between operations  15 us (11%)
  blocking collectives  14.5 us (10%)
  local copies, waits for them, and re-layouts  9.02 us (6%)
  starting transfers between devices  8.65 us (6%)
  other arithmetic  5.54 us (4%)
  matrix products  5.16 us (4%)
    all_gather x1, waiting for transfers between devices, body(): lax.all_gather(summed[:, query_cols:].astype(jnp.bfloat16), ('row', 'col'...  49.1 us
    reduce_scatter x1, waiting for transfers between devices, body(): lax.psum_scatter(partial_value + jnp.concatenate([adapter_term, jnp.zeros...  32.3 us
    all_gather x1, blocking collectives, body(): gathered = lax.all_gather(hidden_states, 'row', axis=0, tiled=True)  14.5 us
    all_to_all x1, starting transfers between devices, body(): lax.all_to_all(outgoing, 'dp', split_axis=0, concat_axis=0, tiled=True)  8.57 us
  transfers between devices with their start and end apart: 3, of which 2 were waited for; matrix products, arithmetic and copies ran while one was open for 2% of the time, Pallas kernels for 0%

commit v1 on v0

--- a/solution.py
+++ b/solution.py
@@ -7,6 +7,28 @@
 HEAD_DIM = 128
 MOST_LEN = 160
 masked_score = -1e30
+
+
+def joined_along(blocks, dim):
+    dims = list(blocks.shape[1:])
+    dims[dim] *= blocks.shape[0]
+    return jnp.moveaxis(blocks, 0, dim).reshape(dims)
+
+
+def collect(shard, axis, dim):
+    count = lax.axis_size(axis)
+    pairs = [(i, (i + 1) % count) for i in range(count)]
+    back = [(b, a) for a, b in pairs]
+    lower, upper = ([], [])
+    for step in range(count - 1):
+        if step % 2 == 0:
+            lower.append(lax.ppermute(lower[-1] if lower else shard, axis, pairs))
+        else:
+            upper.append(lax.ppermute(upper[-1] if upper else shard, axis, back))
+    blocks = jnp.stack([*lower[::-1], shard, *upper])
+    shift = lax.axis_index(axis) - len(lower)
+    blocks = blocks[(jnp.arange(count) - shift) % count]
+    return joined_along(blocks, dim)
 
 
 def block_layout(lengths_row, block_len):
@@ -69,7 +91,7 @@
     block_index = lax.axis_index("dp")
     col_index = lax.axis_index("col")
     row_index = lax.axis_index("row")
-    gathered = lax.all_gather(hidden_states, "row", axis=0, tiled=True)
+    gathered = collect(hidden_states, "row", 0)
     block_len = gathered.shape[0]
     query_cols = w_query.shape[1]
     kv_cols = w_key_value.shape[1]

time: 140 us -> 134 us (0.957)
  blocking collectives: 14.5 us -> 0 us
  waiting for transfers between devices: 81.5 us -> 86.4 us
  starting transfers between devices: 8.65 us -> 12.4 us
    all_gather x1 -> x0, blocking collectives: 14.5 us -> none  [body(): gathered = lax.all_gather(hidden_states, 'row', axis=0, tiled=True)]
    ppermute x0 -> x3, waiting for transfers between devices: none -> 8.06 us  [the longest x2 8.05 us: collect(): lower.append(lax.ppermute(lower[-1] if lower else shard, axis, pairs))]
    reduce_scatter x1, waiting for transfers between devices: 32.3 us -> 28.5 us  [body(): lax.psum_scatter(partial_value + jnp.concatenate([adapter_term, jnp.zeros...]
    ppermute x0 -> x3, starting transfers between devices: none -> 3.76 us  [the longest x2 2.1 us: collect(): lower.append(lax.ppermute(lower[-1] if lower else shard, axis, pairs))]
    reshape x1 -> x0, local copies, waits for them, and re-layouts: 1.85 us -> none  [body(): kv_pieces.reshape(lax.axis_size('row'), lax.axis_size('col'), own_rows, k...]
    all_to_all x1, waiting for transfers between devices: 0.01 us -> 1.51 us  [body(): lax.all_to_all(outgoing, 'dp', split_axis=0, concat_axis=0, tiled=True)]
  transfers between devices with their start and end apart: 3 -> 6, of which waited for: 2 -> 4; matrix products, arithmetic and copies ran while one was open for 2% -> 6% of each run, Pallas kernels for 0% -> 0%
where the time goes in v1:
time: 134 us; the launch traced here: 133 us
  waiting for transfers between devices  86.4 us (64%)
  between operations  15 us (11%)
  starting transfers between devices  12.4 us (9%)
  local copies, waits for them, and re-layouts  8.73 us (7%)
  other arithmetic  5.62 us (4%)
  matrix products  5.2 us (4%)
    all_gather x1, waiting for transfers between devices, body(): lax.all_gather(summed[:, query_cols:].astype(jnp.bfloat16), ('row', 'col'...  48.3 us
    reduce_scatter x1, waiting for transfers between devices, body(): lax.psum_scatter(partial_value + jnp.concatenate([adapter_term, jnp.zeros...  28.5 us
    all_to_all x1, starting transfers between devices, body(): lax.all_to_all(outgoing, 'dp', split_axis=0, concat_axis=0, tiled=True)  8.57 us
    ppermute x2, waiting for transfers between devices, collect(): lower.append(lax.ppermute(lower[-1] if lower else shard, axis, pairs))  8.05 us
  transfers between devices with their start and end apart: 6, of which 4 were waited for; matrix products, arithmetic and copies ran while one was open for 6% of the time, Pallas kernels for 0%

profile of v1, /device:TPU:2, one launch (start us, length us, event | category | flops | bytes accessed | tf_op | source)
XLA Modules:
  0.0 133.4 jit_solution(2715863369448770258)
XLA Ops:
  7.2 1.7 %collective-permute-start = (bf16[256,384]{1,0:T(8,128)(2,1)}, bf16[256,384]{1,0:T(8,128)(2,1)S(1)}, u32[]{:S(2)}, u32[]{:S(2)}) collective-permute-start(bf16[256,384]{1,0:T(8,128)(2,1)} %param.7), channel_id=1, source_target_pairs={{0,64},{64,128},{128,192},{192,0},{1,65},{65,129},{129,193},{193,1... | collective-permute-start | bytes 589832 | tf_op jit(solution)/shard_map/ppermute | solution.py:25
  8.9 1.7 %collective-permute-start.2 = (bf16[256,384]{1,0:T(8,128)(2,1)}, bf16[256,384]{1,0:T(8,128)(2,1)S(1)}, u32[]{:S(2)}, u32[]{:S(2)}) collective-permute-start(bf16[256,384]{1,0:T(8,128)(2,1)} %param.7), channel_id=1, source_target_pairs={{64,0},{128,64},{192,128},{0,192},{65,1},{129,65},{193,129},{1,193... | collective-permute-start | bytes 589832 | tf_op jit(solution)/shard_map/ppermute | solution.py:27
  10.5 0.7 fusion.24
  11.9 1.7 %gather_fusion.1 = bf16[16,384,16]{1,2,0:T(8,128)(2,1)S(1)} fusion(bf16[64,384,16]{1,2,0:T(8,128)(2,1)} %param.10, s32[1024]{0:T(1024)S(1)} %pad_clamp_fusion), kind=kCustom, calls=%fused_computation.1 | custom fusion | bytes 393280 | tf_op jit(solution)/shard_map/jit(_take)/gather | solution.py:118
  13.8 0.8 pad_maximum_fusion.1
  14.6 8.6 %all-to-all-start = ((bf16[16,32,384]{2,1,0:T(8,128)(2,1)}), bf16[16,32,384]{2,1,0:T(8,128)(2,1)S(1)}, u32[]{:S(2)}, u32[]{:S(2)}) async-start(bf16[16,32,384]{2,1,0:T(8,128)(2,1)} %pad_maximum_fusion.1), calls=%async_computation | async-start | bytes 786432 | tf_op jit(solution)/shard_map/all_to_all | solution.py:121
  23.3 0.7 fusion.35
  24.9 0.9 constant_dynamic-slice_fusion.2
  26.4 8.1 %collective-permute-done.1 = bf16[256,384]{1,0:T(8,128)(2,1)S(1)} collective-permute-done((bf16[256,384]{1,0:T(8,128)(2,1)S(1)}, bf16[256,384]{1,0:T(8,128)(2,1)S(1)}, u32[]{:S(2)}, u32[]{:S(2)}) %collective-permute-start.1) | collective-permute-done | bytes 196640 | tf_op jit(solution)/shard_map/ppermute | solution.py:25
  34.6 0.7 gather_fusion
  35.3 1.5 %all-to-all-done = bf16[16,32,384]{2,1,0:T(8,128)(2,1)S(1)} async-done(((bf16[16,32,384]{2,1,0:T(8,128)(2,1)}), bf16[16,32,384]{2,1,0:T(8,128)(2,1)S(1)}, u32[]{:S(2)}, u32[]{:S(2)}) %all-to-all-start) | async-done | bytes 393248 | tf_op jit(solution)/shard_map/all_to_all | solution.py:121
  37.3 1.0 fusion.37
  38.3 2.1 %pad_add_fusion = f32[1024,512]{1,0:T(8,128)} fusion(f32[1024,384]{1,0:T(8,128)S(1)} %fusion.37, bf16[1024,384]{1,0:T(8,128)(2,1)S(1)} %bitcast.65, bf16[384,128]{1,0:T(8,128)(2,1)S(1)} %constant_dynamic-slice_fusion.2, bf16[384,384]{1,0:T(8,128)(2,1)S(1)} %copy-done.1), kind=kOutput, calls=%fused_computation.8 | convolution fusion | flops 403963904 | bytes 4849664 | tf_op jit(solution)/shard_map/dot_general | solution.py:141
  40.5 28.5 %reduce-scatter.2.cloned.1.call-done = f32[256,512]{1,0:T(8,128)} async-done(((f32[1024,512]{1,0:T(8,128)}), f32[256,512]{1,0:T(8,128)}) %reduce-scatter.2.cloned.1.call-update) | async-done | bytes 524304 | tf_op jit(solution)/shard_map/reduce_scatter | solution.py:142
  68.9 1.1 convert.4
  70.8 0.8 fusion.9
  71.8 48.3 %all-gather.3.cloned.1.call-done = bf16[4096,128]{1,0:T(8,128)(2,1)} async-done(((bf16[256,128]{1,0:T(8,128)(2,1)}), bf16[4096,128]{1,0:T(8,128)(2,1)}) %all-gather.3.cloned.1.call-update) | async-done | bytes 1048592 | tf_op jit(solution)/shard_map/all_gather | solution.py:153
  120.1 1.0 dynamic-slice_bitcast_fusion
  121.3 0.8 copy.34
  122.1 1.1 constant_dynamic-slice_fusion.1
  123.2 0.7 fusion
  123.9 0.8 fusion.1
  124.7 1.0 fusion.13
  125.7 0.8 copy.33
  (43 shorter events, 3.4 us)
Async XLA Ops:
  7.2 4.1 %copy-start = (bf16[64,16,384]{2,1,0:T(8,128)(2,1)S(1)}, bf16[64,16,384]{2,1,0:T(8,128)(2,1)}, u32[]{:S(2)}) copy-start(bf16[64,16,384]{2,1,0:T(8,128)(2,1)} %param.11) | copy-start | bytes 2359300
  7.2 27.2 %copy-start.2 = (bf16[256,384]{1,0:T(8,128)(2,1)S(1)}, bf16[256,384]{1,0:T(8,128)(2,1)}, u32[]{:S(2)}) copy-start(bf16[256,384]{1,0:T(8,128)(2,1)} %param.7) | copy-start | bytes 589828
  7.2 16.1 %copy-start.3 = (s32[16,8]{0,1:T(8,128)S(1)}, s32[16,8]{0,1:T(8,128)}, u32[]{:S(2)}) copy-start(s32[16,8]{0,1:T(8,128)} %param.13) | copy-start | bytes 1540
  7.2 16.1 %copy-start.4 = (s32[16,8]{0,1:T(8,128)S(1)}, s32[16,8]{0,1:T(8,128)}, u32[]{:S(2)}) copy-start(s32[16,8]{0,1:T(8,128)} %param.12) | copy-start | bytes 1540
  7.2 18.7 %collective-permute-start = (bf16[256,384]{1,0:T(8,128)(2,1)}, bf16[256,384]{1,0:T(8,128)(2,1)S(1)}, u32[]{:S(2)}, u32[]{:S(2)}) collective-permute-start(bf16[256,384]{1,0:T(8,128)(2,1)} %param.7), channel_id=1, source_target_pairs={{0,64},{64,128},{128,192},{192,0},{1,65},{65,129},{129,193},{193,1... | collective-permute-start | bytes 589832 | tf_op jit(solution)/shard_map/ppermute | solution.py:25
  8.9 17.5 %collective-permute-start.2 = (bf16[256,384]{1,0:T(8,128)(2,1)}, bf16[256,384]{1,0:T(8,128)(2,1)S(1)}, u32[]{:S(2)}, u32[]{:S(2)}) collective-permute-start(bf16[256,384]{1,0:T(8,128)(2,1)} %param.7), channel_id=1, source_target_pairs={{64,0},{128,64},{192,128},{0,192},{65,1},{129,65},{193,129},{1,193... | collective-permute-start | bytes 589832 | tf_op jit(solution)/shard_map/ppermute | solution.py:27
  14.6 22.2 %all-to-all-start = ((bf16[16,32,384]{2,1,0:T(8,128)(2,1)}), bf16[16,32,384]{2,1,0:T(8,128)(2,1)S(1)}, u32[]{:S(2)}, u32[]{:S(2)}) async-start(bf16[16,32,384]{2,1,0:T(8,128)(2,1)} %pad_maximum_fusion.1), calls=%async_computation | async-start | bytes 786432 | tf_op jit(solution)/shard_map/all_to_all | solution.py:121
  23.2 45.8 %reduce-scatter.2.cloned.1.call-start = ((), (), s32[]{:S(2)}) async-start(), calls=%async_computation.2 | async-start | bytes 2621440 | tf_op jit(solution)/shard_map/reduce_scatter | solution.py:142
  25.9 8.5 %collective-permute-start.1 = (bf16[256,384]{1,0:T(8,128)(2,1)S(1)}, bf16[256,384]{1,0:T(8,128)(2,1)S(1)}, u32[]{:S(2)}, u32[]{:S(2)}) collective-permute-start(bf16[256,384]{1,0:T(8,128)(2,1)S(1)} %collective-permute-done), channel_id=1, source_target_pairs={{0,64},{64,128},{128,192},{192,0},{1,65},{65,129},{129,193},{193,1... | collective-permute-start | bytes 589832 | tf_op jit(solution)/shard_map/ppermute | solution.py:25
  35.3 3.0 %copy-start.1 = (bf16[384,384]{1,0:T(8,128)(2,1)S(1)}, bf16[384,384]{1,0:T(8,128)(2,1)}, u32[]{:S(2)}) copy-start(bf16[384,384]{1,0:T(8,128)(2,1)} %param.8) | copy-start | bytes 884740
  40.4 79.7 %all-gather.3.cloned.1.call-start = ((), (), s32[]{:S(2)}) async-start(), calls=%async_computation.3 | async-start | bytes 1114112 | tf_op jit(solution)/shard_map/all_gather | solution.py:153
Sparse Core Ops, SparseCore 0:
  40.5 28.3 reduce-scatter.1
  71.9 48.1 all-gather.2
